TPU v7x, 1024 devices: a whole 8x8x8 slice. The times are simulated.
1024 devices in a mesh: batch: 8 (over z), seq: 8 (over x), head: 16 (over y, core).
Axes of the slice: x: 8, y: 8, z: 8, core: 2. Of those that a mesh axis runs over, the one named last changes fastest.
Arguments:
- queries: bfloat16 [40960, 8192], P(('batch', 'seq', 'head')), parts along dimension 0, may hold values from -6 to 6
- keys: bfloat16 [40960, 8192], P(('batch', 'seq', 'head')), parts along dimension 0, may hold values from -6 to 6
- values: bfloat16 [40960, 8192], P(('batch', 'seq', 'head')), parts along dimension 0, may hold values from -6 to 6
- group_order: int32 [64, 2], P(('batch', 'seq')), parts along dimension 0, may hold values from 0 to 15, as said below
- gain: float32 [8192], P('head'), may hold values from 0.1 to 1.9
Outputs:
- attended: bfloat16 [40960, 8192], P(('batch', 'seq'), 'head'), parts along dimension 0
There are 8 independent parts, one for each index of `batch`. A program takes and returns all parts, laid end to end along the dimension named above; an argument that names none is the same for every part. Nothing has to cross between parts.
Inputs may be any that keep to these rules, and one draw needn't show every extreme that they name: `group_order`: row d holds d and 15 - d, in either order.
All inputs are finite; a program needn't handle non-finite values.
Results may differ from a plain program's by a relative error of at most 0.01.
Values may be sent and summed in bfloat16 or wider, within the bound.
No kernel may reach another device: no remote copies, remote signals or barrier semaphores. Data moves between devices by JAX's collectives and lax.ppermute only.
A program may use at most 32 MiB of HBM per device.

v0:
```python
import jax
import jax.numpy as jnp
from jax import lax
from jax.sharding import PartitionSpec as P

DH = 128


def exchange(lows, both, here, pairs):
    up = lows.astype(jnp.float32)
    down = both.astype(jnp.float32)
    step = 1
    while step < pairs:
        if 2 * step == pairs:
            msg = jnp.where(here + step < pairs, up, down).astype(jnp.bfloat16)
            got = lax.ppermute(
                msg, "seq", [(i, (i + step) % pairs) for i in range(pairs)]
            ).astype(jnp.float32)
            up = up + jnp.where(here >= step, got, 0.0)
            down = down + jnp.where(here + step < pairs, got, 0.0)
        else:
            got_up = lax.ppermute(
                up.astype(jnp.bfloat16), "seq", [(i, i + step) for i in range(pairs - step)]
            )
            got_down = lax.ppermute(
                down.astype(jnp.bfloat16), "seq", [(i, i - step) for i in range(step, pairs)]
            )
            up = up + got_up.astype(jnp.float32)
            down = down + got_down.astype(jnp.float32)
        step *= 2
    low_sum = up - lows.astype(jnp.float32)
    high_sum = low_sum + (down - both.astype(jnp.float32))
    return low_sum, high_sum


def local(queries, keys, values, group_order, gain):
    rows_in, feats = keys.shape
    ndev = lax.axis_size("head")
    width = feats // ndev
    local_heads = gain.shape[0] // DH
    groups = 1
    gh = local_heads // groups
    rows = ndev * rows_in
    half = rows // 2
    pairs = lax.axis_size("seq")
    here = lax.axis_index("seq")
    order = group_order[0]
    low_first = order[0] < pairs

    def by_dest(x):
        return x.reshape(rows_in, ndev, width).transpose(1, 0, 2)

    kd = by_dest(keys).reshape(ndev, rows_in, groups, gh * DH)
    vd = by_dest(values).reshape(ndev, rows_in, groups, gh * DH)
    tie = ()
    kx_parts, vx_parts, pre_parts = [], [], []
    for g in range(groups):
        kv = jnp.stack([kd[:, :, g], vd[:, :, g]], axis=1).reshape(ndev, 2 * rows_in, gh * DH)
        if tie:
            kv, tie = lax.optimization_barrier((kv, tie))
            pre_parts.append(exchange(*tie, here, pairs))
        kv_all = lax.all_to_all(kv, "head", split_axis=0, concat_axis=0, tiled=True)
        kv_all = kv_all.reshape(ndev, 2, rows_in, gh * DH)
        kx = kv_all[:, 0].reshape(rows, gh, DH)
        vx = kv_all[:, 1].reshape(rows, gh, DH)
        kx_parts.append(kx)
        vx_parts.append(vx)
        kh = kx.reshape(2, half, gh, DH)
        vh = vx.reshape(2, half, gh, DH)
        state = jnp.einsum("jthd,jthe->jhde", kh, vh, preferred_element_type=jnp.float32).astype(
            jnp.bfloat16
        )
        lows = jnp.where(low_first, state[0], state[1])
        highs = jnp.where(low_first, state[1], state[0])
        both = (lows.astype(jnp.float32) + highs.astype(jnp.float32)).astype(jnp.bfloat16)
        tie = (lows, both)
    q_in, tie = lax.optimization_barrier((by_dest(queries), tie))
    pre_parts.append(exchange(*tie, here, pairs))
    q_all = lax.all_to_all(q_in, "head", split_axis=0, concat_axis=0, tiled=True)
    qx = q_all.reshape(rows, local_heads, DH)
    kx = jnp.concatenate(kx_parts, axis=1)
    vx = jnp.concatenate(vx_parts, axis=1)
    low_sum = jnp.concatenate([p[0] for p in pre_parts], axis=0)
    high_sum = jnp.concatenate([p[1] for p in pre_parts], axis=0)
    first_pre = jnp.where(low_first, low_sum, high_sum).astype(jnp.bfloat16)
    second_pre = jnp.where(low_first, high_sum, low_sum).astype(jnp.bfloat16)
    index = jnp.arange(rows, dtype=jnp.int32)
    position = order[index // half] * half + index % half
    scores = jnp.einsum("thd,shd->hts", qx, kx, preferred_element_type=jnp.float32)
    allowed = position[:, None] >= position[None, :]
    scores = jnp.where(allowed[None], scores, 0.0).astype(jnp.bfloat16)
    intra = jnp.einsum("hts,she->the", scores, vx, preferred_element_type=jnp.float32)
    intra = lax.optimization_barrier(intra)
    qh = qx.reshape(2, half, local_heads, DH)
    first_term = jnp.einsum("thd,hde->the", qh[0], first_pre, preferred_element_type=jnp.float32)
    second_term = jnp.einsum("thd,hde->the", qh[1], second_pre, preferred_element_type=jnp.float32)
    raw = intra + jnp.concatenate([first_term, second_term], axis=0)
    scale = lax.rsqrt(jnp.mean(raw * raw, axis=-1, keepdims=True) + 1e-06)
    gains = gain.reshape(local_heads, DH)
    return (raw * scale * gains).astype(jnp.bfloat16).reshape(rows, local_heads * DH)


def solution(mesh):
    return jax.shard_map(
        local,
        mesh=mesh,
        in_specs=(
            P(("batch", "seq", "head"), None),
            P(("batch", "seq", "head"), None),
            P(("batch", "seq", "head"), None),
            P(("batch", "seq"), None),
            P("head"),
        ),
        out_specs=P(("batch", "seq"), "head"),
        check_vma=False,
    )
```

profile of v0, /device:TPU:2, one launch (start us, length us, event | category | flops | bytes accessed | tf_op | source)
XLA Modules:
  0.0 93.3 jit_solution(14750847816462758749)
XLA Ops:
  0.0 1.4 %bitcast_bitcast_fusion.1 = (bf16[16,1,40,512]{3,2,1,0:T(8,128)(2,1)S(1)}, bf16[16,1,40,512]{3,2,1,0:T(8,128)(2,1)S(1)}) fusion(bf16[5,16,8,512]{3,2,1,0:T(8,128)(2,1)} %bitcast.50, bf16[5,16,8,512]{3,2,1,0:T(8,128)(2,1)} %bitcast.51), kind=kLoop, calls=%fused_computation.15 | loop fusion | bytes 2621440 | tf_op jit(solution)/shard_map/stack;squeeze;reshape | solution.py:58
  1.4 1.2 %pad_maximum_fusion = bf16[16,2,40,512]{3,2,1,0:T(8,128)(2,1)} fusion(bf16[16,1,40,512]{3,2,1,0:T(8,128)(2,1)S(1)} %get-tuple-element.19, bf16[16,1,40,512]{3,2,1,0:T(8,128)(2,1)S(1)} %get-tuple-element.20), kind=kLoop, calls=%fused_computation.6 | loop fusion | flops 655360 | bytes 2621440 | tf_op jit(solution)/shard_map/stack | solution.py:58
  2.6 7.8 %all-to-all-start = ((bf16[16,80,512]{2,1,0:T(8,128)(2,1)}), bf16[16,80,512]{2,1,0:T(8,128)(2,1)S(1)}, u32[]{:S(2)}, u32[]{:S(2)}) async-start(bf16[16,80,512]{2,1,0:T(8,128)(2,1)} %bitcast.4), calls=%async_computation | async-start | bytes 2621440 | tf_op jit(solution)/shard_map/all_to_all | solution.py:62
  10.4 0.9 copy.46
  11.3 0.6 fusion.37
  12.5 30.0 %all-to-all-done = bf16[16,80,512]{2,1,0:T(8,128)(2,1)S(1)} async-done(((bf16[16,80,512]{2,1,0:T(8,128)(2,1)}), bf16[16,80,512]{2,1,0:T(8,128)(2,1)S(1)}, u32[]{:S(2)}, u32[]{:S(2)}) %all-to-all-start) | async-done | bytes 1310752 | tf_op jit(solution)/shard_map/all_to_all | solution.py:62
  42.6 0.2 reshape_reshape_squeeze.7
  42.8 0.2 reshape_reshape_squeeze.6
  42.9 0.4 convolution_convert_fusion
  43.5 4.9 %all-to-all-start.1 = ((bf16[16,40,512]{2,1,0:T(8,128)(2,1)}), bf16[16,40,512]{2,1,0:T(8,128)(2,1)S(1)}, u32[]{:S(2)}, u32[]{:S(2)}) async-start(bf16[16,40,512]{2,1,0:T(8,128)(2,1)} %bitcast.47), calls=%async_computation.1 | async-start | bytes 1310720 | tf_op jit(solution)/shard_map/all_to_all | solution.py:79
  48.4 1.2 %fusion.31 = s32[640]{0:T(1024)S(1)} fusion(s32[]{:T(128)} %bitcast.7, s32[]{:T(128)} %bitcast.6), kind=kLoop, calls=%fused_computation.60 | loop fusion | flops 8960 | bytes 2568 | tf_op jit(solution)/shard_map/mul | solution.py:88
  49.6 3.4 %collective-permute-start = (bf16[4,128,128]{2,1,0:T(8,128)(2,1)S(1)}, bf16[4,128,128]{2,1,0:T(8,128)(2,1)S(1)}, u32[]{:S(2)}, u32[]{:S(2)}) collective-permute-start(bf16[4,128,128]{2,1,0:T(8,128)(2,1)S(1)} %get-tuple-element.9), channel_id=1, source_target_pairs={{0,16},{16,32},{32,48},{48,64},{64,80},{80,96},{96,112},{1,17},{17... | collective-permute-start | bytes 393224 | tf_op jit(solution)/shard_map/ppermute | solution.py:22
  53.0 8.9 %collective-permute-start.2 = (bf16[4,128,128]{2,1,0:T(8,128)(2,1)S(1)}, bf16[4,128,128]{2,1,0:T(8,128)(2,1)S(1)}, u32[]{:S(2)}, u32[]{:S(2)}) collective-permute-start(bf16[4,128,128]{2,1,0:T(8,128)(2,1)S(1)} %get-tuple-element.10), channel_id=1, source_target_pairs={{16,0},{32,16},{48,32},{64,48},{80,64},{96,80},{112,96},{17,1},{33... | collective-permute-start | bytes 393224 | tf_op jit(solution)/shard_map/ppermute | solution.py:25
  62.0 2.1 %collective-permute-done = bf16[4,128,128]{2,1,0:T(8,128)(2,1)S(1)} collective-permute-done((bf16[4,128,128]{2,1,0:T(8,128)(2,1)S(1)}, bf16[4,128,128]{2,1,0:T(8,128)(2,1)S(1)}, u32[]{:S(2)}, u32[]{:S(2)}) %collective-permute-start) | collective-permute-done | bytes 131104 | tf_op jit(solution)/shard_map/ppermute | solution.py:22
  64.1 1.3 %collective-permute-start.1 = (bf16[4,128,128]{2,1,0:T(8,128)(2,1)S(1)}, bf16[4,128,128]{2,1,0:T(8,128)(2,1)S(1)}, u32[]{:S(2)}, u32[]{:S(2)}) collective-permute-start(bf16[4,128,128]{2,1,0:T(8,128)(2,1)S(1)} %fusion.20), channel_id=1, source_target_pairs={{0,32},{16,48},{32,64},{48,80},{64,96},{80,112},{1,33},{17,49},{33... | collective-permute-start | bytes 393224 | tf_op jit(solution)/shard_map/ppermute | solution.py:22
  65.4 0.7 fusion.21
  66.1 1.3 %collective-permute-start.3 = (bf16[4,128,128]{2,1,0:T(8,128)(2,1)}, bf16[4,128,128]{2,1,0:T(8,128)(2,1)S(1)}, u32[]{:S(2)}, u32[]{:S(2)}) collective-permute-start(bf16[4,128,128]{2,1,0:T(8,128)(2,1)} %fusion.21), channel_id=1, source_target_pairs={{32,0},{48,16},{64,32},{80,48},{96,64},{112,80},{33,1},{49,17},{65... | collective-permute-start | bytes 393224 | tf_op jit(solution)/shard_map/ppermute | solution.py:25
  67.4 1.1 %broadcast_compare_fusion = pred[640,640]{1,0:T(8,128)(4,1)} fusion(s32[640]{0:T(1024)S(1)} %fusion.26), kind=kLoop, calls=%fused_computation.13 | loop fusion | flops 409600 | bytes 412160 | tf_op jit(solution)/shard_map/ge | solution.py:90
  68.6 1.0 %reshape_squeeze.6 = bf16[640,4,128]{2,1,0:T(4,128)(2,1)} reshape(bf16[16,1,40,512]{3,2,1,0:T(8,128)(2,1)S(1)} %get-tuple-element.13) | data formatting | bytes 1310720 | tf_op jit(solution)/shard_map/reshape;squeeze | solution.py:65
  69.6 0.6 collective-permute-done.1
  70.2 6.8 %collective-permute-done.3 = bf16[4,128,128]{2,1,0:T(8,128)(2,1)S(1)} collective-permute-done((bf16[4,128,128]{2,1,0:T(8,128)(2,1)}, bf16[4,128,128]{2,1,0:T(8,128)(2,1)S(1)}, u32[]{:S(2)}, u32[]{:S(2)}) %collective-permute-start.3) | collective-permute-done | bytes 131104 | tf_op jit(solution)/shard_map/ppermute | solution.py:25
  77.0 0.8 select_convert_fusion.4
  77.8 1.9 %collective-permute-start.4 = (bf16[4,128,128]{2,1,0:T(8,128)(2,1)}, bf16[4,128,128]{2,1,0:T(8,128)(2,1)S(1)}, u32[]{:S(2)}, u32[]{:S(2)}) collective-permute-start(bf16[4,128,128]{2,1,0:T(8,128)(2,1)} %select_convert_fusion.4), channel_id=1, source_target_pairs={{0,64},{16,80},{32,96},{48,112},{64,0},{80,16},{96,32},{112,48},{1... | collective-permute-start | bytes 393224 | tf_op jit(solution)/shard_map/ppermute | solution.py:16
  79.7 1.0 %reshape.142 = bf16[640,4,128]{2,1,0:T(4,128)(2,1)} reshape(bf16[16,40,512]{2,1,0:T(8,128)(2,1)S(1)} %all-to-all-done.1) | data formatting | bytes 1310720 | tf_op jit(solution)/shard_map/reshape | solution.py:80
  80.7 3.4 %fusion.5 = f32[640,4,128]{0,2,1:T(8,128)S(1)} fusion(pred[640,640]{1,0:T(8,128)(4,1)} %broadcast_compare_fusion, bf16[640,4,128]{2,1,0:T(4,128)(2,1)S(1)} %reshape_squeeze.7, bf16[640,4,128]{2,1,0:T(4,128)(2,1)} %reshape.142, bf16[640,4,128]{2,1,0:T(4,128)(2,1)} %reshape_squeeze.6), kind=kOutput, calls=%fused_computation.5 | convolution fusion | flops 842137600 | bytes 3686400 | tf_op jit(solution)/shard_map/hts,she->the/dot_general | solution.py:92
  84.3 6.0 %collective-permute-done.4 = bf16[4,128,128]{2,1,0:T(8,128)(2,1)S(1)} collective-permute-done((bf16[4,128,128]{2,1,0:T(8,128)(2,1)}, bf16[4,128,128]{2,1,0:T(8,128)(2,1)S(1)}, u32[]{:S(2)}, u32[]{:S(2)}) %collective-permute-start.4) | collective-permute-done | bytes 131104 | tf_op jit(solution)/shard_map/ppermute | solution.py:16
  90.2 0.4 convolution_bitcast_fusion
  90.6 0.4 convolution_bitcast_fusion.1
  91.0 0.4 multiply_reduce_fusion
  91.4 0.3 copy-done.1
  91.7 0.4 multiply_convert_fusion
  92.2 1.1 %copy.19 = bf16[640,512]{1,0:T(8,128)(2,1)} copy(bf16[640,512]{0,1:T(8,128)(2,1)S(1)} %bitcast.49) | data formatting | bytes 1310720 | tf_op jit(solution)/shard_map/reshape | solution.py:100
  (16 shorter events, 0.6 us)
Async XLA Ops:
  2.6 7.8 %copy-start = (bf16[40,8192]{1,0:T(8,128)(2,1)S(1)}, bf16[40,8192]{1,0:T(8,128)(2,1)}, u32[]{:S(2)}) copy-start(bf16[40,8192]{1,0:T(8,128)(2,1)} %param.5) | copy-start | bytes 1966084
  2.6 39.9 %all-to-all-start = ((bf16[16,80,512]{2,1,0:T(8,128)(2,1)}), bf16[16,80,512]{2,1,0:T(8,128)(2,1)S(1)}, u32[]{:S(2)}, u32[]{:S(2)}) async-start(bf16[16,80,512]{2,1,0:T(8,128)(2,1)} %bitcast.4), calls=%async_computation | async-start | bytes 2621440 | tf_op jit(solution)/shard_map/all_to_all | solution.py:62
  10.4 0.9 copy-start.2
  43.5 36.2 %all-to-all-start.1 = ((bf16[16,40,512]{2,1,0:T(8,128)(2,1)}), bf16[16,40,512]{2,1,0:T(8,128)(2,1)S(1)}, u32[]{:S(2)}, u32[]{:S(2)}) async-start(bf16[16,40,512]{2,1,0:T(8,128)(2,1)} %bitcast.47), calls=%async_computation.1 | async-start | bytes 1310720 | tf_op jit(solution)/shard_map/all_to_all | solution.py:79
  49.6 14.5 %collective-permute-start = (bf16[4,128,128]{2,1,0:T(8,128)(2,1)S(1)}, bf16[4,128,128]{2,1,0:T(8,128)(2,1)S(1)}, u32[]{:S(2)}, u32[]{:S(2)}) collective-permute-start(bf16[4,128,128]{2,1,0:T(8,128)(2,1)S(1)} %get-tuple-element.9), channel_id=1, source_target_pairs={{0,16},{16,32},{32,48},{48,64},{64,80},{80,96},{96,112},{1,17},{17... | collective-permute-start | bytes 393224 | tf_op jit(solution)/shard_map/ppermute | solution.py:22
  53.0 12.4 %collective-permute-start.2 = (bf16[4,128,128]{2,1,0:T(8,128)(2,1)S(1)}, bf16[4,128,128]{2,1,0:T(8,128)(2,1)S(1)}, u32[]{:S(2)}, u32[]{:S(2)}) collective-permute-start(bf16[4,128,128]{2,1,0:T(8,128)(2,1)S(1)} %get-tuple-element.10), channel_id=1, source_target_pairs={{16,0},{32,16},{48,32},{64,48},{80,64},{96,80},{112,96},{17,1},{33... | collective-permute-start | bytes 393224 | tf_op jit(solution)/shard_map/ppermute | solution.py:25
  64.1 6.1 %collective-permute-start.1 = (bf16[4,128,128]{2,1,0:T(8,128)(2,1)S(1)}, bf16[4,128,128]{2,1,0:T(8,128)(2,1)S(1)}, u32[]{:S(2)}, u32[]{:S(2)}) collective-permute-start(bf16[4,128,128]{2,1,0:T(8,128)(2,1)S(1)} %fusion.20), channel_id=1, source_target_pairs={{0,32},{16,48},{32,64},{48,80},{64,96},{80,112},{1,33},{17,49},{33... | collective-permute-start | bytes 393224 | tf_op jit(solution)/shard_map/ppermute | solution.py:22
  66.1 10.9 %collective-permute-start.3 = (bf16[4,128,128]{2,1,0:T(8,128)(2,1)}, bf16[4,128,128]{2,1,0:T(8,128)(2,1)S(1)}, u32[]{:S(2)}, u32[]{:S(2)}) collective-permute-start(bf16[4,128,128]{2,1,0:T(8,128)(2,1)} %fusion.21), channel_id=1, source_target_pairs={{32,0},{48,16},{64,32},{80,48},{96,64},{112,80},{33,1},{49,17},{65... | collective-permute-start | bytes 393224 | tf_op jit(solution)/shard_map/ppermute | solution.py:25
  77.8 12.5 %collective-permute-start.4 = (bf16[4,128,128]{2,1,0:T(8,128)(2,1)}, bf16[4,128,128]{2,1,0:T(8,128)(2,1)S(1)}, u32[]{:S(2)}, u32[]{:S(2)}) collective-permute-start(bf16[4,128,128]{2,1,0:T(8,128)(2,1)} %select_convert_fusion.4), channel_id=1, source_target_pairs={{0,64},{16,80},{32,96},{48,112},{64,0},{80,16},{96,32},{112,48},{1... | collective-permute-start | bytes 393224 | tf_op jit(solution)/shard_map/ppermute | solution.py:16
  91.0 0.7 copy-start.1
where the time goes:
time: 93.7 us; the launch traced here: 93.3 us
  waiting for transfers between devices  45.5 us (49%)
  starting transfers between devices  29.5 us (31%)
  local copies, waits for them, and re-layouts  6.99 us (7%)
  other arithmetic  5.86 us (6%)
  matrix products  4.57 us (5%)
    all_to_all x1, waiting for transfers between devices, local(): kv_all = lax.all_to_all(kv, 'head', split_axis=0, concat_axis=0, tiled=True)  30 us
    ppermute x2, starting transfers between devices, exchange(): lax.ppermute(down.astype(jnp.bfloat16), 'seq', [(i, i - step) for i in ra...  10.2 us
    all_to_all x1, starting transfers between devices, local(): kv_all = lax.all_to_all(kv, 'head', split_axis=0, concat_axis=0, tiled=True)  7.79 us
    ppermute x2, waiting for transfers between devices, exchange(): lax.ppermute(down.astype(jnp.bfloat16), 'seq', [(i, i - step) for i in ra...  6.79 us
    ppermute x1, waiting for transfers between devices, exchange(): lax.ppermute(msg, 'seq', [(i, (i + step) % pairs) for i in range(pairs)])  5.98 us
    all_to_all x1, starting transfers between devices, local(): lax.all_to_all(q_in, 'head', split_axis=0, concat_axis=0, tiled=True)  4.92 us
    ppermute x2, starting transfers between devices, exchange(): lax.ppermute(up.astype(jnp.bfloat16), 'seq', [(i, i + step) for i in rang...  4.7 us
    dot_general x1, matrix products, local(): jnp.einsum('hts,she->the', scores, vx, preferred_element_type=jnp.float32)  3.36 us
  transfers between devices with their start and end apart: 7, of which 5 were waited for; matrix products, arithmetic and copies ran while one was open for 12% of the time, Pallas kernels for 0%

commit v1 on v0

--- a/solution.py
+++ b/solution.py
@@ -9,7 +9,13 @@
 def exchange(lows, both, here, pairs):
     up = lows.astype(jnp.float32)
     down = both.astype(jnp.float32)
-    step = 1
+    reach = pairs // 2
+    for step in range(1, reach):
+        got_up = lax.ppermute(lows, "seq", [(i, i + step) for i in range(pairs - step)])
+        got_down = lax.ppermute(both, "seq", [(i, i - step) for i in range(step, pairs)])
+        up = up + got_up.astype(jnp.float32)
+        down = down + got_down.astype(jnp.float32)
+    step = reach
     while step < pairs:
         if 2 * step == pairs:
             msg = jnp.where(here + step < pairs, up, down).astype(jnp.bfloat16)

time: 93.7 us -> 109 us (1.16)
  the two profiles are of different devices: /device:TPU:2 before, /device:TPU:1 now
where the time goes in v1:
time: 109 us; the launch traced here: 108 us
  starting transfers between devices  56 us (51%)
  waiting for transfers between devices  32.3 us (30%)
  local copies, waits for them, and re-layouts  7.87 us (7%)
  matrix products  6.6 us (6%)
  other arithmetic  4.52 us (4%)
    all_to_all x1, waiting for transfers between devices, local(): kv_all = lax.all_to_all(kv, 'head', split_axis=0, concat_axis=0, tiled=True)  31.2 us
    all_to_all x1, starting transfers between devices, local(): kv_all = lax.all_to_all(kv, 'head', split_axis=0, concat_axis=0, tiled=True)  17.7 us
    ppermute x3, starting transfers between devices, exchange(): lax.ppermute(lows, 'seq', [(i, i + step) for i in range(pairs - step)])  15.9 us
    ppermute x1, starting transfers between devices, exchange(): lax.ppermute(msg, 'seq', [(i, (i + step) % pairs) for i in range(pairs)])  14.7 us
    ppermute x3, starting transfers between devices, exchange(): lax.ppermute(both, 'seq', [(i, i - step) for i in range(step, pairs)])  3.88 us
    all_to_all x1, starting transfers between devices, local(): lax.all_to_all(q_in, 'head', split_axis=0, concat_axis=0, tiled=True)  3.8 us
    dot_general x1, matrix products, local(): jnp.einsum('hts,she->the', scores, vx, preferred_element_type=jnp.float32)  3.45 us
  transfers between devices with their start and end apart: 9, of which 2 were waited for; matrix products, arithmetic and copies ran while one was open for 10% of the time, Pallas kernels for 0%

profile of v1, /device:TPU:1, one launch (start us, length us, event | category | flops | bytes accessed | tf_op | source)
XLA Modules:
  0.0 108.2 jit_solution(6093256649531289907)
XLA Ops:
  0.0 1.4 %bitcast_bitcast_fusion.1 = (bf16[16,1,40,512]{3,2,1,0:T(8,128)(2,1)S(1)}, bf16[16,1,40,512]{3,2,1,0:T(8,128)(2,1)S(1)}) fusion(bf16[5,16,8,512]{3,2,1,0:T(8,128)(2,1)} %bitcast.50, bf16[5,16,8,512]{3,2,1,0:T(8,128)(2,1)} %bitcast.51), kind=kLoop, calls=%fused_computation.15 | loop fusion | bytes 2621440 | tf_op jit(solution)/shard_map/stack;squeeze;reshape | solution.py:64
  1.4 1.2 %pad_maximum_fusion = bf16[16,2,40,512]{3,2,1,0:T(8,128)(2,1)} fusion(bf16[16,1,40,512]{3,2,1,0:T(8,128)(2,1)S(1)} %get-tuple-element.19, bf16[16,1,40,512]{3,2,1,0:T(8,128)(2,1)S(1)} %get-tuple-element.20), kind=kLoop, calls=%fused_computation.6 | loop fusion | flops 655360 | bytes 2621440 | tf_op jit(solution)/shard_map/stack | solution.py:64
  2.6 17.7 %all-to-all-start = ((bf16[16,80,512]{2,1,0:T(8,128)(2,1)}), bf16[16,80,512]{2,1,0:T(8,128)(2,1)S(1)}, u32[]{:S(2)}, u32[]{:S(2)}) async-start(bf16[16,80,512]{2,1,0:T(8,128)(2,1)} %bitcast.4), calls=%async_computation | async-start | bytes 2621440 | tf_op jit(solution)/shard_map/all_to_all | solution.py:68
  20.4 0.9 copy.46
  21.3 0.6 fusion.37
  22.5 31.2 %all-to-all-done = bf16[16,80,512]{2,1,0:T(8,128)(2,1)S(1)} async-done(((bf16[16,80,512]{2,1,0:T(8,128)(2,1)}), bf16[16,80,512]{2,1,0:T(8,128)(2,1)S(1)}, u32[]{:S(2)}, u32[]{:S(2)}) %all-to-all-start) | async-done | bytes 1310752 | tf_op jit(solution)/shard_map/all_to_all | solution.py:68
  53.6 0.1 fusion.35
  53.8 0.2 reshape_reshape_squeeze.7
  53.9 0.2 reshape_reshape_squeeze.6
  54.1 0.4 convolution_convert_fusion
  54.6 3.8 %all-to-all-start.1 = ((bf16[16,40,512]{2,1,0:T(8,128)(2,1)}), bf16[16,40,512]{2,1,0:T(8,128)(2,1)S(1)}, u32[]{:S(2)}, u32[]{:S(2)}) async-start(bf16[16,40,512]{2,1,0:T(8,128)(2,1)} %bitcast.47), calls=%async_computation.1 | async-start | bytes 1310720 | tf_op jit(solution)/shard_map/all_to_all | solution.py:85
  58.4 1.3 %fusion.33 = s32[640]{0:T(1024)S(1)} fusion(s32[]{:T(128)} %bitcast.7, s32[]{:T(128)} %bitcast.6), kind=kLoop, calls=%fused_computation.60 | loop fusion | flops 8960 | bytes 2568 | tf_op jit(solution)/shard_map/mul | solution.py:94
  59.7 1.3 %collective-permute-start.5 = (bf16[4,128,128]{2,1,0:T(8,128)(2,1)S(1)}, bf16[4,128,128]{2,1,0:T(8,128)(2,1)S(1)}, u32[]{:S(2)}, u32[]{:S(2)}) collective-permute-start(bf16[4,128,128]{2,1,0:T(8,128)(2,1)S(1)} %get-tuple-element.10), channel_id=1, source_target_pairs={{48,0},{64,16},{80,32},{96,48},{112,64},{49,1},{65,17},{81,33},{97... | collective-permute-start | bytes 393224 | tf_op jit(solution)/shard_map/ppermute | solution.py:15
  61.0 1.3 %collective-permute-start.4 = (bf16[4,128,128]{2,1,0:T(8,128)(2,1)S(1)}, bf16[4,128,128]{2,1,0:T(8,128)(2,1)S(1)}, u32[]{:S(2)}, u32[]{:S(2)}) collective-permute-start(bf16[4,128,128]{2,1,0:T(8,128)(2,1)S(1)} %get-tuple-element.10), channel_id=1, source_target_pairs={{32,0},{48,16},{64,32},{80,48},{96,64},{112,80},{33,1},{49,17},{65... | collective-permute-start | bytes 393224 | tf_op jit(solution)/shard_map/ppermute | solution.py:15
  62.3 1.3 %collective-permute-start.3 = (bf16[4,128,128]{2,1,0:T(8,128)(2,1)S(1)}, bf16[4,128,128]{2,1,0:T(8,128)(2,1)S(1)}, u32[]{:S(2)}, u32[]{:S(2)}) collective-permute-start(bf16[4,128,128]{2,1,0:T(8,128)(2,1)S(1)} %get-tuple-element.10), channel_id=1, source_target_pairs={{16,0},{32,16},{48,32},{64,48},{80,64},{96,80},{112,96},{17,1},{33... | collective-permute-start | bytes 393224 | tf_op jit(solution)/shard_map/ppermute | solution.py:15
  63.6 7.0 %collective-permute-start.2 = (bf16[4,128,128]{2,1,0:T(8,128)(2,1)S(1)}, bf16[4,128,128]{2,1,0:T(8,128)(2,1)S(1)}, u32[]{:S(2)}, u32[]{:S(2)}) collective-permute-start(bf16[4,128,128]{2,1,0:T(8,128)(2,1)S(1)} %get-tuple-element.9), channel_id=1, source_target_pairs={{0,48},{16,64},{32,80},{48,96},{64,112},{1,49},{17,65},{33,81},{49... | collective-permute-start | bytes 393224 | tf_op jit(solution)/shard_map/ppermute | solution.py:14
  70.7 5.5 %collective-permute-start.1 = (bf16[4,128,128]{2,1,0:T(8,128)(2,1)S(1)}, bf16[4,128,128]{2,1,0:T(8,128)(2,1)S(1)}, u32[]{:S(2)}, u32[]{:S(2)}) collective-permute-start(bf16[4,128,128]{2,1,0:T(8,128)(2,1)S(1)} %get-tuple-element.9), channel_id=1, source_target_pairs={{0,32},{16,48},{32,64},{48,80},{64,96},{80,112},{1,33},{17,49},{33... | collective-permute-start | bytes 393224 | tf_op jit(solution)/shard_map/ppermute | solution.py:14
  76.2 3.4 %collective-permute-start = (bf16[4,128,128]{2,1,0:T(8,128)(2,1)S(1)}, bf16[4,128,128]{2,1,0:T(8,128)(2,1)S(1)}, u32[]{:S(2)}, u32[]{:S(2)}) collective-permute-start(bf16[4,128,128]{2,1,0:T(8,128)(2,1)S(1)} %get-tuple-element.9), channel_id=1, source_target_pairs={{0,16},{16,32},{32,48},{48,64},{64,80},{80,96},{96,112},{1,17},{17... | collective-permute-start | bytes 393224 | tf_op jit(solution)/shard_map/ppermute | solution.py:14
  79.5 0.3 broadcast_compare_fusion
  79.8 1.0 reshape_squeeze.7
  80.8 1.0 reshape_squeeze.6
  81.9 0.8 select_convert_fusion.4
  82.7 14.7 %collective-permute-start.6 = (bf16[4,128,128]{2,1,0:T(8,128)(2,1)}, bf16[4,128,128]{2,1,0:T(8,128)(2,1)}, u32[]{:S(2)}, u32[]{:S(2)}) collective-permute-start(bf16[4,128,128]{2,1,0:T(8,128)(2,1)} %select_convert_fusion.4), channel_id=1, source_target_pairs={{0,64},{16,80},{32,96},{48,112},{64,0},{80,16},{96,32},{112,48},{1... | collective-permute-start | bytes 393224 | tf_op jit(solution)/shard_map/ppermute | solution.py:22
  97.4 1.0 reshape.142
  98.4 3.4 %fusion.5 = f32[640,4,128]{0,2,1:T(8,128)S(1)} fusion(pred[640,640]{1,0:T(8,128)(4,1)S(1)} %broadcast_compare_fusion, bf16[640,4,128]{2,1,0:T(4,128)(2,1)} %reshape_squeeze.7, bf16[640,4,128]{2,1,0:T(4,128)(2,1)} %reshape.142, bf16[640,4,128]{2,1,0:T(4,128)(2,1)} %reshape_squeeze.6), kind=kOutput, calls=%fused_computation.5 | convolution fusion | flops 842137600 | bytes 3686400 | tf_op jit(solution)/shard_map/hts,she->the/dot_general | solution.py:98
  102.1 1.1 %collective-permute-done.6 = bf16[4,128,128]{2,1,0:T(8,128)(2,1)} collective-permute-done((bf16[4,128,128]{2,1,0:T(8,128)(2,1)}, bf16[4,128,128]{2,1,0:T(8,128)(2,1)}, u32[]{:S(2)}, u32[]{:S(2)}) %collective-permute-start.6) | collective-permute-done | bytes 131104 | tf_op jit(solution)/shard_map/ppermute | solution.py:22
  103.2 1.4 %convolution_bitcast_fusion = f32[320,4,128]{0,2,1:T(8,128)S(1)} fusion(bf16[320,4,128]{2,1,0:T(4,128)(2,1)S(1)} %squeeze.16, pred[]{:T(512)} %bitcast.9, bf16[4,128,128]{2,1,0:T(8,128)(2,1)S(1)} %get-tuple-element.9, bf16[4,128,128]{2,1,0:T(8,128)(2,1)} %collective-permute-done.6, bf16[4,128,128]{2,1,0:T(8,128)(2,1)S(1)} %collective-permute-done.2, ...), kind=kOutput, calls=%fused_computation.10 | convolution fusion | flops 43515904 | bytes 2162691 | tf_op jit(solution)/shard_map/thd,hde->the/dot_general | solution.py:102
  104.6 1.3 %convolution_bitcast_fusion.1 = f32[320,4,128]{0,2,1:T(8,128)S(1)} fusion(bf16[320,4,128]{2,1,0:T(4,128)(2,1)S(1)} %squeeze.7, pred[]{:T(512)} %bitcast.9, bf16[4,128,128]{2,1,0:T(8,128)(2,1)S(1)} %get-tuple-element.9, bf16[4,128,128]{2,1,0:T(8,128)(2,1)} %collective-permute-done.6, bf16[4,128,128]{2,1,0:T(8,128)(2,1)S(1)} %collective-permute-done.2, ...), kind=kOutput, calls=%fused_computation.11 | convolution fusion | flops 43515904 | bytes 2162691 | tf_op jit(solution)/shard_map/thd,hde->the/dot_general | solution.py:101
  106.0 0.4 multiply_reduce_fusion
  106.4 0.3 copy-done.3
  106.7 0.4 multiply_convert_fusion
  107.1 1.1 %copy.19 = bf16[640,512]{1,0:T(8,128)(2,1)} copy(bf16[640,512]{0,1:T(8,128)(2,1)S(1)} %bitcast.49) | data formatting | bytes 1310720 | tf_op jit(solution)/shard_map/reshape | solution.py:106
  (22 shorter events, 0.3 us)
Async XLA Ops:
  2.6 17.7 %copy-start.2 = (bf16[40,8192]{1,0:T(8,128)(2,1)S(1)}, bf16[40,8192]{1,0:T(8,128)(2,1)}, u32[]{:S(2)}) copy-start(bf16[40,8192]{1,0:T(8,128)(2,1)} %param.5) | copy-start | bytes 1966084
  2.6 51.0 %all-to-all-start = ((bf16[16,80,512]{2,1,0:T(8,128)(2,1)}), bf16[16,80,512]{2,1,0:T(8,128)(2,1)S(1)}, u32[]{:S(2)}, u32[]{:S(2)}) async-start(bf16[16,80,512]{2,1,0:T(8,128)(2,1)} %bitcast.4), calls=%async_computation | async-start | bytes 2621440 | tf_op jit(solution)/shard_map/all_to_all | solution.py:68
  20.3 0.9 copy-start.4
  54.6 42.8 %all-to-all-start.1 = ((bf16[16,40,512]{2,1,0:T(8,128)(2,1)}), bf16[16,40,512]{2,1,0:T(8,128)(2,1)S(1)}, u32[]{:S(2)}, u32[]{:S(2)}) async-start(bf16[16,40,512]{2,1,0:T(8,128)(2,1)} %bitcast.47), calls=%async_computation.1 | async-start | bytes 1310720 | tf_op jit(solution)/shard_map/all_to_all | solution.py:85
  59.7 16.5 %collective-permute-start.5 = (bf16[4,128,128]{2,1,0:T(8,128)(2,1)S(1)}, bf16[4,128,128]{2,1,0:T(8,128)(2,1)S(1)}, u32[]{:S(2)}, u32[]{:S(2)}) collective-permute-start(bf16[4,128,128]{2,1,0:T(8,128)(2,1)S(1)} %get-tuple-element.10), channel_id=1, source_target_pairs={{48,0},{64,16},{80,32},{96,48},{112,64},{49,1},{65,17},{81,33},{97... | collective-permute-start | bytes 393224 | tf_op jit(solution)/shard_map/ppermute | solution.py:15
  61.0 20.8 %collective-permute-start.4 = (bf16[4,128,128]{2,1,0:T(8,128)(2,1)S(1)}, bf16[4,128,128]{2,1,0:T(8,128)(2,1)S(1)}, u32[]{:S(2)}, u32[]{:S(2)}) collective-permute-start(bf16[4,128,128]{2,1,0:T(8,128)(2,1)S(1)} %get-tuple-element.10), channel_id=1, source_target_pairs={{32,0},{48,16},{64,32},{80,48},{96,64},{112,80},{33,1},{49,17},{65... | collective-permute-start | bytes 393224 | tf_op jit(solution)/shard_map/ppermute | solution.py:15
  62.3 19.5 %collective-permute-start.3 = (bf16[4,128,128]{2,1,0:T(8,128)(2,1)S(1)}, bf16[4,128,128]{2,1,0:T(8,128)(2,1)S(1)}, u32[]{:S(2)}, u32[]{:S(2)}) collective-permute-start(bf16[4,128,128]{2,1,0:T(8,128)(2,1)S(1)} %get-tuple-element.10), channel_id=1, source_target_pairs={{16,0},{32,16},{48,32},{64,48},{80,64},{96,80},{112,96},{17,1},{33... | collective-permute-start | bytes 393224 | tf_op jit(solution)/shard_map/ppermute | solution.py:15
  63.6 18.3 %collective-permute-start.2 = (bf16[4,128,128]{2,1,0:T(8,128)(2,1)S(1)}, bf16[4,128,128]{2,1,0:T(8,128)(2,1)S(1)}, u32[]{:S(2)}, u32[]{:S(2)}) collective-permute-start(bf16[4,128,128]{2,1,0:T(8,128)(2,1)S(1)} %get-tuple-element.9), channel_id=1, source_target_pairs={{0,48},{16,64},{32,80},{48,96},{64,112},{1,49},{17,65},{33,81},{49... | collective-permute-start | bytes 393224 | tf_op jit(solution)/shard_map/ppermute | solution.py:14
  70.7 11.2 %collective-permute-start.1 = (bf16[4,128,128]{2,1,0:T(8,128)(2,1)S(1)}, bf16[4,128,128]{2,1,0:T(8,128)(2,1)S(1)}, u32[]{:S(2)}, u32[]{:S(2)}) collective-permute-start(bf16[4,128,128]{2,1,0:T(8,128)(2,1)S(1)} %get-tuple-element.9), channel_id=1, source_target_pairs={{0,32},{16,48},{32,64},{48,80},{64,96},{80,112},{1,33},{17,49},{33... | collective-permute-start | bytes 393224 | tf_op jit(solution)/shard_map/ppermute | solution.py:14
  76.2 5.7 %collective-permute-start = (bf16[4,128,128]{2,1,0:T(8,128)(2,1)S(1)}, bf16[4,128,128]{2,1,0:T(8,128)(2,1)S(1)}, u32[]{:S(2)}, u32[]{:S(2)}) collective-permute-start(bf16[4,128,128]{2,1,0:T(8,128)(2,1)S(1)} %get-tuple-element.9), channel_id=1, source_target_pairs={{0,16},{16,32},{32,48},{48,64},{64,80},{80,96},{96,112},{1,17},{17... | collective-permute-start | bytes 393224 | tf_op jit(solution)/shard_map/ppermute | solution.py:14
  81.9 16.5 %copy-start = (bf16[4,128,128]{2,1,0:T(8,128)(2,1)}, bf16[4,128,128]{2,1,0:T(8,128)(2,1)S(1)}, u32[]{:S(2)}) copy-start(bf16[4,128,128]{2,1,0:T(8,128)(2,1)S(1)} %collective-permute-done) | copy-start | bytes 393220
  82.7 20.5 %collective-permute-start.6 = (bf16[4,128,128]{2,1,0:T(8,128)(2,1)}, bf16[4,128,128]{2,1,0:T(8,128)(2,1)}, u32[]{:S(2)}, u32[]{:S(2)}) collective-permute-start(bf16[4,128,128]{2,1,0:T(8,128)(2,1)} %select_convert_fusion.4), channel_id=1, source_target_pairs={{0,64},{16,80},{32,96},{48,112},{64,0},{80,16},{96,32},{112,48},{1... | collective-permute-start | bytes 393224 | tf_op jit(solution)/shard_map/ppermute | solution.py:22
  102.1 2.5 %copy-start.1 = (bf16[4,128,128]{2,1,0:T(8,128)(2,1)S(1)}, bf16[4,128,128]{2,1,0:T(8,128)(2,1)}, u32[]{:S(2)}) copy-start(bf16[4,128,128]{2,1,0:T(8,128)(2,1)} %copy-done) | copy-start | bytes 393220
  106.0 0.7 copy-start.3
